TPU v7x, 512 devices: a whole 4x8x8 slice. The times are simulated.
512 devices in a mesh: row: 16 (over y, x_lo), col: 16 (over z, core), ka: 2 (over x_hi).
Axes of the slice: x: 4 (x_hi: 2, x_lo: 2; x = x_hi * 2 + x_lo), y: 8, z: 8, core: 2. Of those that a mesh axis runs over, the one named last changes fastest.
Arguments:
- pair: bfloat16 [512, 512, 128], P('row', ('col', 'ka')), may hold values from -6 to 6
- pair_mask: int32 [512, 512], P('row', ('col', 'ka')), may hold values from 0 to 1, as said below
- w_in: bfloat16 [2, 128, 512], replicated, may hold values from -0.5 to 0.5
- w_gate: bfloat16 [2, 128, 128], replicated, may hold values from -0.5 to 0.5
- w_out: bfloat16 [2, 128, 128], replicated, may hold values from -0.5 to 0.5
Outputs:
- updated: bfloat16 [512, 512, 128], P('row', ('col', 'ka'))
Inputs may be any that keep to these rules, and one draw needn't show every extreme that they name: pair_mask[i, j] = v[i] v[j] for a per-token 0/1 validity v; within each aligned run of 16 tokens the real tokens come first and there is at least one.
All inputs are finite; a program needn't handle non-finite values.
Results may differ from a plain program's by a relative error of at most 0.014.
Values may be sent and summed in bfloat16 or wider, within the bound.
No kernel may reach another device: no remote copies, remote signals or barrier semaphores. Data moves between devices by JAX's collectives and lax.ppermute only.
A program may use at most 64 MiB of HBM per device.

v0:
```python
import jax
import jax.numpy as jnp
from jax import lax
from jax.sharding import PartitionSpec as P


def layer_norm(value):
    mean = jnp.mean(value, axis=-1, keepdims=True)
    centred = value - mean
    var = jnp.mean(centred * centred, axis=-1, keepdims=True)
    return centred / jnp.sqrt(var + 1e-05)


def prepare(pair, valid, weight_in, weight_gate):
    normed = layer_norm(pair.astype(jnp.float32)).astype(jnp.bfloat16)
    proj = jnp.einsum("ijc,cd->ijd", normed, weight_in, preferred_element_type=jnp.float32)
    width = proj.shape[-1] // 4
    left = (jax.nn.sigmoid(proj[..., :width]) * proj[..., width : 2 * width] * valid).astype(
        jnp.bfloat16
    )
    right = (
        jax.nn.sigmoid(proj[..., 2 * width : 3 * width]) * proj[..., 3 * width :] * valid
    ).astype(jnp.bfloat16)
    gate = jax.nn.sigmoid(
        jnp.einsum("ijc,cd->ijd", normed, weight_gate, preferred_element_type=jnp.float32)
    )
    return (left, right, gate)


def finish(pair, tri, gate, weight_out):
    normed = layer_norm(tri).astype(jnp.bfloat16)
    proj = jnp.einsum("ijc,cd->ijd", normed, weight_out, preferred_element_type=jnp.float32)
    return (pair.astype(jnp.float32) + gate * proj).astype(jnp.bfloat16)


def transpose_tiles(value, n):
    perm = [(r * n + c, c * n + r) for r in range(n) for c in range(n)]
    return lax.ppermute(value, ("row", "col"), perm)


def on_device(n, pair, pair_mask, w_in, w_gate, w_out):
    valid = pair_mask.astype(jnp.float32)[..., None]
    left, right, gate = prepare(pair, valid, w_in[0], w_gate[0])
    left_rows = lax.all_gather(left, "col", axis=1, tiled=True)
    right_diag = lax.all_gather(transpose_tiles(right, n), "row", axis=1, tiled=True)
    partial_value = jnp.einsum(
        "ikc,jkc->ijc", left_rows, right_diag, preferred_element_type=jnp.float32
    )
    tri = lax.psum_scatter(
        partial_value.astype(jnp.bfloat16), "ka", scatter_dimension=1, tiled=True
    ).astype(jnp.float32)
    middle = finish(pair, tri, gate, w_out[0])
    left, right, gate = prepare(middle, valid, w_in[1], w_gate[1])
    right_cols = lax.all_gather(right, "row", axis=0, tiled=True)
    left_half = lax.all_gather(transpose_tiles(left, n), "col", axis=0, tiled=True)
    left_diag = lax.all_gather(left_half, "ka", axis=1, tiled=True)
    tri = jnp.einsum("kic,kjc->ijc", left_diag, right_cols, preferred_element_type=jnp.float32)
    return finish(middle, tri, gate, w_out[1])


def solution(mesh):
    n = mesh.shape["row"]
    assert mesh.shape["col"] == n
    placed = (P("row", ("col", "ka"), None), P("row", ("col", "ka")), P(), P(), P())
    return jax.shard_map(
        lambda *a: on_device(n, *a),
        mesh=mesh,
        in_specs=placed,
        out_specs=P("row", ("col", "ka"), None),
        check_vma=False,
    )
```

profile of v0, /device:TPU:1, one launch (start us, length us, event | category | flops | bytes accessed | tf_op | source)
XLA Modules:
  0.0 423.1 jit_solution(14155994391619889289)
XLA Ops:
  6.5 1.0 convert_reduce_fusion.1
  7.7 1.1 fusion.18
  9.8 1.3 fusion.42
  12.1 4.5 %collective-permute-start = (bf16[32,16,128]{2,1,0:T(8,128)(2,1)S(1)}, bf16[32,16,128]{2,1,0:T(8,128)(2,1)S(1)}, u32[]{:S(2)}, u32[]{:S(2)}) collective-permute-start(bf16[32,16,128]{2,1,0:T(8,128)(2,1)S(1)} %get-tuple-element.8), channel_id=1, source_target_pairs={{0,0},{2,32},{4,64},{6,96},{8,128},{10,160},{12,192},{14,224},{16,... | collective-permute-start | bytes 393224 | tf_op jit(solution)/shard_map/ppermute | solution.py:38
  16.6 2.6 collective-permute-done
  19.9 45.1 %all-gather.8.cloned.1.call-done = bf16[32,256,128]{2,1,0:T(8,128)(2,1)} async-done(((bf16[32,16,128]{2,1,0:T(8,128)(2,1)}), bf16[32,256,128]{2,1,0:T(8,128)(2,1)}) %all-gather.8.cloned.1.call-update) | async-done | bytes 2097168 | tf_op jit(solution)/shard_map/all_gather | solution.py:44
  65.1 15.2 %copy.49 = bf16[32,256,128]{0,1,2:T(8,128)(2,1)} copy(bf16[32,256,128]{2,1,0:T(8,128)(2,1)} %all-gather.8.cloned.1.call-done) | data formatting | bytes 4194304 | tf_op jit(solution)/shard_map/all_gather | solution.py:44
  80.3 57.6 %all-gather.6.cloned.1.call-done = bf16[32,256,128]{2,1,0:T(8,128)(2,1)} async-done(((bf16[32,16,128]{2,1,0:T(8,128)(2,1)}), bf16[32,256,128]{2,1,0:T(8,128)(2,1)}) %all-gather.6.cloned.1.call-update) | async-done | bytes 2097168 | tf_op jit(solution)/shard_map/all_gather | solution.py:45
  137.9 15.2 %copy.48 = bf16[32,256,128]{0,1,2:T(8,128)(2,1)} copy(bf16[32,256,128]{2,1,0:T(8,128)(2,1)} %all-gather.6.cloned.1.call-done) | data formatting | bytes 4194304 | tf_op jit(solution)/shard_map/all_gather | solution.py:45
  153.2 9.2 %fusion = bf16[32,32,128]{0,1,2:T(8,128)(2,1)} fusion(bf16[32,256,128]{0,1,2:T(8,128)(2,1)} %copy.48, bf16[32,256,128]{0,1,2:T(8,128)(2,1)} %copy.49), kind=kOutput, calls=%fused_computation.1 | convolution fusion | flops 67239936 | bytes 4456448 | tf_op jit(solution)/shard_map/ikc,jkc->ijc/dot_general | solution.py:46
  162.8 39.5 %reduce-scatter.2.cloned.1.call-done = bf16[32,16,128]{0,1,2:T(8,128)(2,1)} async-done(((bf16[32,32,128]{0,1,2:T(8,128)(2,1)}), bf16[32,16,128]{0,1,2:T(8,128)(2,1)}) %reduce-scatter.2.cloned.1.call-update) | async-done | bytes 131088 | tf_op jit(solution)/shard_map/reduce_scatter | solution.py:49
  202.3 1.2 convert_reduce_fusion
  203.5 1.3 fusion.14
  204.8 1.2 fusion.15
  207.7 0.8 fusion.21
  208.5 2.9 collective-permute-start.1
  211.4 3.4 collective-permute-done.1
  216.1 53.4 %all-gather.12.cloned.1.call-done = bf16[512,16,128]{2,1,0:T(8,128)(2,1)} async-done(((bf16[32,16,128]{2,1,0:T(8,128)(2,1)}), bf16[512,16,128]{2,1,0:T(8,128)(2,1)}) %all-gather.12.cloned.1.call-update) | async-done | bytes 2097168 | tf_op jit(solution)/shard_map/all_gather | solution.py:55
  269.5 4.9 %copy.55 = bf16[512,16,128]{0,1,2:T(8,128)(2,1)} copy(bf16[512,16,128]{2,1,0:T(8,128)(2,1)} %all-gather.12.cloned.1.call-done) | data formatting | bytes 4194304 | tf_op jit(solution)/shard_map/all_gather | solution.py:55
  274.8 59.3 %all-gather.10.cloned.1.call-done = bf16[512,16,128]{2,1,0:T(8,128)(2,1)} async-done(((bf16[32,16,128]{2,1,0:T(8,128)(2,1)}), bf16[512,16,128]{2,1,0:T(8,128)(2,1)}) %all-gather.10.cloned.1.call-update) | async-done | bytes 2097168 | tf_op jit(solution)/shard_map/all_gather | solution.py:54
  334.1 3.9 copy.56
  338.0 73.1 %all-gather.14.cloned.1.call-done = bf16[512,32,128]{0,1,2:T(8,128)(2,1)} async-done(((bf16[512,16,128]{0,1,2:T(8,128)(2,1)}), bf16[512,32,128]{0,1,2:T(8,128)(2,1)}) %all-gather.14.cloned.1.call-update) | async-done | bytes 4194320 | tf_op jit(solution)/shard_map/all_gather | solution.py:56
  411.1 3.4 fusion.57
  415.4 0.8 fusion.13
  (52 shorter events, 7.3 us)
Async XLA Ops:
  6.5 58.5 %all-gather.8.cloned.1.call-start = ((), (), s32[]{:S(2)}) async-start(), calls=%async_computation.2 | async-start | bytes 2228224 | tf_op jit(solution)/shard_map/all_gather | solution.py:44
  12.0 125.9 %all-gather.6.cloned.1.call-start = ((), (), s32[]{:S(2)}) async-start(), calls=%async_computation.1 | async-start | bytes 2228224 | tf_op jit(solution)/shard_map/all_gather | solution.py:45
  12.1 7.1 %collective-permute-start = (bf16[32,16,128]{2,1,0:T(8,128)(2,1)S(1)}, bf16[32,16,128]{2,1,0:T(8,128)(2,1)S(1)}, u32[]{:S(2)}, u32[]{:S(2)}) collective-permute-start(bf16[32,16,128]{2,1,0:T(8,128)(2,1)S(1)} %get-tuple-element.8), channel_id=1, source_target_pairs={{0,0},{2,32},{4,64},{6,96},{8,128},{10,160},{12,192},{14,224},{16,... | collective-permute-start | bytes 393224 | tf_op jit(solution)/shard_map/ppermute | solution.py:38
  19.2 0.7 copy-start.3
  19.9 182.4 %reduce-scatter.2.cloned.1.call-start = ((), (), s32[]{:S(2)}) async-start(), calls=%async_computation.3 | async-start | bytes 1572864 | tf_op jit(solution)/shard_map/reduce_scatter | solution.py:49
  153.2 9.3 %copy-start = (bf16[32,16,128]{2,1,0:T(8,128)(2,1)S(1)}, bf16[32,16,128]{2,1,0:T(8,128)(2,1)}, u32[]{:S(2)}) copy-start(bf16[32,16,128]{2,1,0:T(8,128)(2,1)} %param.5) | copy-start | bytes 393220
  153.2 9.3 %copy-start.5 = (bf16[2,128,128]{2,1,0:T(8,128)(2,1)S(1)}, bf16[2,128,128]{2,1,0:T(8,128)(2,1)}, u32[]{:S(2)}) copy-start(bf16[2,128,128]{2,1,0:T(8,128)(2,1)} %param.8) | copy-start | bytes 196612
  162.3 44.1 %copy-start.4 = (bf16[2,128,128]{2,1,0:T(8,128)(2,1)S(1)}, bf16[2,128,128]{2,1,0:T(8,128)(2,1)}, u32[]{:S(2)}) copy-start(bf16[2,128,128]{2,1,0:T(8,128)(2,1)} %param.9) | copy-start | bytes 196612
  162.3 45.0 %copy-start.1 = (bf16[2,128,512]{2,1,0:T(8,128)(2,1)S(1)}, bf16[2,128,512]{2,1,0:T(8,128)(2,1)}, u32[]{:S(2)}) copy-start(bf16[2,128,512]{2,1,0:T(8,128)(2,1)} %param.7) | copy-start | bytes 786436
  162.4 107.2 %all-gather.12.cloned.1.call-start = ((), (), s32[]{:S(2)}) async-start(), calls=%async_computation.5 | async-start | bytes 2228224 | tf_op jit(solution)/shard_map/all_gather | solution.py:55
  208.5 6.3 %collective-permute-start.1 = (bf16[32,16,128]{2,1,0:T(8,128)(2,1)S(1)}, bf16[32,16,128]{2,1,0:T(8,128)(2,1)S(1)}, u32[]{:S(2)}, u32[]{:S(2)}) collective-permute-start(bf16[32,16,128]{2,1,0:T(8,128)(2,1)S(1)} %get-tuple-element.5), channel_id=1, source_target_pairs={{0,0},{2,32},{4,64},{6,96},{8,128},{10,160},{12,192},{14,224},{16,... | collective-permute-start | bytes 393224 | tf_op jit(solution)/shard_map/ppermute | solution.py:38
  214.8 0.6 copy-start.2
  215.5 118.6 %all-gather.10.cloned.1.call-start = ((), (), s32[]{:S(2)}) async-start(), calls=%async_computation.4 | async-start | bytes 2228224 | tf_op jit(solution)/shard_map/all_gather | solution.py:54
  216.1 195.1 %all-gather.14.cloned.1.call-start = ((), (), s32[]{:S(2)}) async-start(), calls=%async_computation.6 | async-start | bytes 6291456 | tf_op jit(solution)/shard_map/all_gather | solution.py:56
Sparse Core Ops, SparseCore 0:
  12.1 52.8 all-gather.7
  67.1 70.8 all-gather.5
  162.5 39.7 reduce-scatter.1
  215.6 53.8 all-gather.11
  271.5 62.6 all-gather.9
  336.1 75.0 all-gather.13
where the time goes:
time: 424 us; the launch traced here: 423 us
  waiting for transfers between devices  335 us (79%)
  local copies, waits for them, and re-layouts  42.3 us (10%)
  matrix products  16 us (4%)
  between operations  13.6 us (3%)
  other arithmetic  8.84 us (2%)
  starting transfers between devices  7.61 us (2%)
    all_gather x1, waiting for transfers between devices, on_device(): left_diag = lax.all_gather(left_half, 'ka', axis=1, tiled=True)  73.1 us
    all_gather x1, waiting for transfers between devices, on_device(): right_cols = lax.all_gather(right, 'row', axis=0, tiled=True)  59.3 us
    all_gather x1, waiting for transfers between devices, on_device(): lax.all_gather(transpose_tiles(right, n), 'row', axis=1, tiled=True)  57.6 us
    all_gather x1, waiting for transfers between devices, on_device(): lax.all_gather(transpose_tiles(left, n), 'col', axis=0, tiled=True)  53.4 us
    all_gather x1, waiting for transfers between devices, on_device(): left_rows = lax.all_gather(left, 'col', axis=1, tiled=True)  45.1 us
    reduce_scatter x1, waiting for transfers between devices, on_device(): lax.psum_scatter(partial_value.astype(jnp.bfloat16), 'ka', scatter_dimens...  39.5 us
    all_gather x1, local copies, waits for them, and re-layouts, on_device(): left_rows = lax.all_gather(left, 'col', axis=1, tiled=True)  15.2 us
    all_gather x1, local copies, waits for them, and re-layouts, on_device(): lax.all_gather(transpose_tiles(right, n), 'row', axis=1, tiled=True)  15.2 us
  transfers between devices with their start and end apart: 8, of which 8 were waited for; matrix products, arithmetic and copies ran while one was open for 6% of the time, Pallas kernels for 0%

commit v1 on v0

--- a/solution.py
+++ b/solution.py
@@ -41,7 +41,9 @@
 def on_device(n, pair, pair_mask, w_in, w_gate, w_out):
     valid = pair_mask.astype(jnp.float32)[..., None]
     left, right, gate = prepare(pair, valid, w_in[0], w_gate[0])
-    left_rows = lax.all_gather(left, "col", axis=1, tiled=True)
+    left_rows = jnp.concatenate(
+        lax.all_to_all(jnp.stack([left] * lax.axis_size("col")), "col", 0, 0), axis=1
+    )
     right_diag = lax.all_gather(transpose_tiles(right, n), "row", axis=1, tiled=True)
     partial_value = jnp.einsum(
         "ikc,jkc->ijc", left_rows, right_diag, preferred_element_type=jnp.float32

time: 424 us -> 394 us (0.929)
  waiting for transfers between devices: 335 us -> 305 us
  starting transfers between devices: 7.61 us -> 19.6 us
  local copies, waits for them, and re-layouts: 42.3 us -> 34.1 us
    all_to_all x0 -> x1, waiting for transfers between devices: none -> 50.9 us  [on_device(): lax.all_to_all(jnp.stack([left] * lax.axis_size('col')), 'col', 0, 0)]
    all_gather x1 -> x0, waiting for transfers between devices: 45.1 us -> none  [on_device(): left_rows = lax.all_gather(left, 'col', axis=1, tiled=True)]
    all_gather x1, waiting for transfers between devices: 57.6 us -> 26 us  [on_device(): lax.all_gather(transpose_tiles(right, n), 'row', axis=1, tiled=True)]
    all_gather x1 -> x0, local copies, waits for them, and re-layouts: 15.2 us -> none  [on_device(): left_rows = lax.all_gather(left, 'col', axis=1, tiled=True)]
    all_to_all x0 -> x1, starting transfers between devices: none -> 12 us  [on_device(): lax.all_to_all(jnp.stack([left] * lax.axis_size('col')), 'col', 0, 0)]
  transfers between devices with their start and end apart: 8 -> 8, of which waited for: 8 -> 7; matrix products, arithmetic and copies ran while one was open for 6% -> 4% of each run, Pallas kernels for 0% -> 0%
where the time goes in v1:
time: 394 us
  waiting for transfers between devices  305 us (77%)
  local copies, waits for them, and re-layouts  34.1 us (9%)
  starting transfers between devices  19.6 us (5%)
  matrix products  13.7 us (3%)
  between operations  13.3 us (3%)
  other arithmetic  8.18 us (2%)
    all_gather x1, waiting for transfers between devices, on_device(): left_diag = lax.all_gather(left_half, 'ka', axis=1, tiled=True)  73.1 us
    all_gather x1, waiting for transfers between devices, on_device(): right_cols = lax.all_gather(right, 'row', axis=0, tiled=True)  59.3 us
    all_gather x1, waiting for transfers between devices, on_device(): lax.all_gather(transpose_tiles(left, n), 'col', axis=0, tiled=True)  53.5 us
    all_to_all x1, waiting for transfers between devices, on_device(): lax.all_to_all(jnp.stack([left] * lax.axis_size('col')), 'col', 0, 0)  50.9 us
    reduce_scatter x1, waiting for transfers between devices, on_device(): lax.psum_scatter(partial_value.astype(jnp.bfloat16), 'ka', scatter_dimens...  37.9 us
    all_gather x1, waiting for transfers between devices, on_device(): lax.all_gather(transpose_tiles(right, n), 'row', axis=1, tiled=True)  26 us
    all_gather x1, local copies, waits for them, and re-layouts, on_device(): lax.all_gather(transpose_tiles(right, n), 'row', axis=1, tiled=True)  15.2 us
    all_to_all x1, starting transfers between devices, on_device(): lax.all_to_all(jnp.stack([left] * lax.axis_size('col')), 'col', 0, 0)  12 us
  transfers between devices with their start and end apart: 8, of which 7 were waited for; matrix products, arithmetic and copies ran while one was open for 4% of the time, Pallas kernels for 0%

profile of v1, /device:TPU:1, one launch (start us, length us, event | category | flops | bytes accessed | tf_op | source)
XLA Modules:
  0.0 393.6 jit_solution(10176634348250687206)
XLA Ops:
  6.5 1.0 convert_reduce_fusion.1
  7.7 1.1 fusion.18
  9.8 1.3 fusion.42
  11.3 4.5 %collective-permute-start = (bf16[32,16,128]{2,1,0:T(8,128)(2,1)S(1)}, bf16[32,16,128]{2,1,0:T(8,128)(2,1)S(1)}, u32[]{:S(2)}, u32[]{:S(2)}) collective-permute-start(bf16[32,16,128]{2,1,0:T(8,128)(2,1)S(1)} %get-tuple-element.8), channel_id=1, source_target_pairs={{0,0},{2,32},{4,64},{6,96},{8,128},{10,160},{12,192},{14,224},{16,... | collective-permute-start | bytes 393224 | tf_op jit(solution)/shard_map/ppermute | solution.py:38
  15.8 1.7 stack.2
  17.6 12.0 %all-to-all-start = ((bf16[16,32,16,128]{3,2,1,0:T(8,128)(2,1)}), bf16[16,32,16,128]{3,2,1,0:T(8,128)(2,1)S(1)}, u32[]{:S(2)}, u32[]{:S(2)}) async-start(bf16[16,32,16,128]{3,2,1,0:T(8,128)(2,1)} %stack.2), calls=%async_computation | async-start | bytes 4194304 | tf_op jit(solution)/shard_map/all_to_all | solution.py:45
  30.4 50.9 %all-to-all-done = bf16[16,32,16,128]{3,2,1,0:T(8,128)(2,1)S(1)} async-done(((bf16[16,32,16,128]{3,2,1,0:T(8,128)(2,1)}), bf16[16,32,16,128]{3,2,1,0:T(8,128)(2,1)S(1)}, u32[]{:S(2)}, u32[]{:S(2)}) %all-to-all-start) | async-done | bytes 2097184 | tf_op jit(solution)/shard_map/all_to_all | solution.py:45
  81.3 1.9 copy.61
  83.2 3.4 copy.63
  86.6 26.0 %all-gather.5.cloned.1.call-done = bf16[32,256,128]{2,1,0:T(8,128)(2,1)} async-done(((bf16[32,16,128]{2,1,0:T(8,128)(2,1)}), bf16[32,256,128]{2,1,0:T(8,128)(2,1)}) %all-gather.5.cloned.1.call-update) | async-done | bytes 2097168 | tf_op jit(solution)/shard_map/all_gather | solution.py:47
  112.7 15.2 %copy.62 = bf16[32,256,128]{0,1,2:T(8,128)(2,1)} copy(bf16[32,256,128]{2,1,0:T(8,128)(2,1)} %all-gather.5.cloned.1.call-done) | data formatting | bytes 4194304 | tf_op jit(solution)/shard_map/all_gather | solution.py:47
  127.9 6.8 %fusion = bf16[32,32,128]{0,1,2:T(8,128)(2,1)} fusion(bf16[32,256,128]{0,1,2:T(8,128)(2,1)} %copy.62, bf16[32,256,128]{1,0,2:T(8,128)(2,1)S(1)} %copy.63), kind=kOutput, calls=%fused_computation.1 | convolution fusion | flops 67239936 | bytes 4456448 | tf_op jit(solution)/shard_map/ikc,jkc->ijc/dot_general | solution.py:48
  135.2 37.9 %reduce-scatter.2.cloned.1.call-done = bf16[32,16,128]{0,1,2:T(8,128)(2,1)} async-done(((bf16[32,32,128]{0,1,2:T(8,128)(2,1)}), bf16[32,16,128]{0,1,2:T(8,128)(2,1)}) %reduce-scatter.2.cloned.1.call-update) | async-done | bytes 131088 | tf_op jit(solution)/shard_map/reduce_scatter | solution.py:51
  173.1 1.2 convert_reduce_fusion
  174.3 1.3 fusion.14
  175.5 1.2 fusion.15
  179.3 2.9 collective-permute-start.1
  182.2 3.4 collective-permute-done.1
  186.9 53.5 %all-gather.9.cloned.1.call-done = bf16[512,16,128]{2,1,0:T(8,128)(2,1)} async-done(((bf16[32,16,128]{2,1,0:T(8,128)(2,1)}), bf16[512,16,128]{2,1,0:T(8,128)(2,1)}) %all-gather.9.cloned.1.call-update) | async-done | bytes 2097168 | tf_op jit(solution)/shard_map/all_gather | solution.py:57
  240.4 4.9 %copy.69 = bf16[512,16,128]{0,1,2:T(8,128)(2,1)} copy(bf16[512,16,128]{2,1,0:T(8,128)(2,1)} %all-gather.9.cloned.1.call-done) | data formatting | bytes 4194304 | tf_op jit(solution)/shard_map/all_gather | solution.py:57
  245.6 59.3 %all-gather.7.cloned.1.call-done = bf16[512,16,128]{2,1,0:T(8,128)(2,1)} async-done(((bf16[32,16,128]{2,1,0:T(8,128)(2,1)}), bf16[512,16,128]{2,1,0:T(8,128)(2,1)}) %all-gather.7.cloned.1.call-update) | async-done | bytes 2097168 | tf_op jit(solution)/shard_map/all_gather | solution.py:56
  304.9 3.9 copy.70
  308.9 73.1 %all-gather.11.cloned.1.call-done = bf16[512,32,128]{0,1,2:T(8,128)(2,1)} async-done(((bf16[512,16,128]{0,1,2:T(8,128)(2,1)}), bf16[512,32,128]{0,1,2:T(8,128)(2,1)}) %all-gather.11.cloned.1.call-update) | async-done | bytes 4194320 | tf_op jit(solution)/shard_map/all_gather | solution.py:58
  382.0 3.4 fusion.57
  (53 shorter events, 8.3 us)
Async XLA Ops:
  11.3 18.3 %collective-permute-start = (bf16[32,16,128]{2,1,0:T(8,128)(2,1)S(1)}, bf16[32,16,128]{2,1,0:T(8,128)(2,1)S(1)}, u32[]{:S(2)}, u32[]{:S(2)}) collective-permute-start(bf16[32,16,128]{2,1,0:T(8,128)(2,1)S(1)} %get-tuple-element.8), channel_id=1, source_target_pairs={{0,0},{2,32},{4,64},{6,96},{8,128},{10,160},{12,192},{14,224},{16,... | collective-permute-start | bytes 393224 | tf_op jit(solution)/shard_map/ppermute | solution.py:38
  17.6 63.7 %all-to-all-start = ((bf16[16,32,16,128]{3,2,1,0:T(8,128)(2,1)}), bf16[16,32,16,128]{3,2,1,0:T(8,128)(2,1)S(1)}, u32[]{:S(2)}, u32[]{:S(2)}) async-start(bf16[16,32,16,128]{3,2,1,0:T(8,128)(2,1)} %stack.2), calls=%async_computation | async-start | bytes 4194304 | tf_op jit(solution)/shard_map/all_to_all | solution.py:45
  29.6 83.0 %all-gather.5.cloned.1.call-start = ((), (), s32[]{:S(2)}) async-start(), calls=%async_computation.2 | async-start | bytes 2228224 | tf_op jit(solution)/shard_map/all_gather | solution.py:47
  29.7 0.7 copy-start.2
  30.4 142.7 %reduce-scatter.2.cloned.1.call-start = ((), (), s32[]{:S(2)}) async-start(), calls=%async_computation.3 | async-start | bytes 1572864 | tf_op jit(solution)/shard_map/reduce_scatter | solution.py:51
  127.9 6.9 %copy-start = (bf16[32,16,128]{2,1,0:T(8,128)(2,1)S(1)}, bf16[32,16,128]{2,1,0:T(8,128)(2,1)}, u32[]{:S(2)}) copy-start(bf16[32,16,128]{2,1,0:T(8,128)(2,1)} %param.5) | copy-start | bytes 393220
  127.9 6.9 %copy-start.5 = (bf16[2,128,128]{2,1,0:T(8,128)(2,1)S(1)}, bf16[2,128,128]{2,1,0:T(8,128)(2,1)}, u32[]{:S(2)}) copy-start(bf16[2,128,128]{2,1,0:T(8,128)(2,1)} %param.8) | copy-start | bytes 196612
  134.8 42.5 %copy-start.4 = (bf16[2,128,128]{2,1,0:T(8,128)(2,1)S(1)}, bf16[2,128,128]{2,1,0:T(8,128)(2,1)}, u32[]{:S(2)}) copy-start(bf16[2,128,128]{2,1,0:T(8,128)(2,1)} %param.9) | copy-start | bytes 196612
  134.8 105.6 %all-gather.9.cloned.1.call-start = ((), (), s32[]{:S(2)}) async-start(), calls=%async_computation.5 | async-start | bytes 2228224 | tf_op jit(solution)/shard_map/all_gather | solution.py:57
  135.2 42.9 %copy-start.1 = (bf16[2,128,512]{2,1,0:T(8,128)(2,1)S(1)}, bf16[2,128,512]{2,1,0:T(8,128)(2,1)}, u32[]{:S(2)}) copy-start(bf16[2,128,512]{2,1,0:T(8,128)(2,1)} %param.7) | copy-start | bytes 786436
  179.3 6.3 %collective-permute-start.1 = (bf16[32,16,128]{2,1,0:T(8,128)(2,1)S(1)}, bf16[32,16,128]{2,1,0:T(8,128)(2,1)S(1)}, u32[]{:S(2)}, u32[]{:S(2)}) collective-permute-start(bf16[32,16,128]{2,1,0:T(8,128)(2,1)S(1)} %get-tuple-element.5), channel_id=1, source_target_pairs={{0,0},{2,32},{4,64},{6,96},{8,128},{10,160},{12,192},{14,224},{16,... | collective-permute-start | bytes 393224 | tf_op jit(solution)/shard_map/ppermute | solution.py:38
  185.6 0.7 copy-start.3
  186.3 118.7 %all-gather.7.cloned.1.call-start = ((), (), s32[]{:S(2)}) async-start(), calls=%async_computation.4 | async-start | bytes 2228224 | tf_op jit(solution)/shard_map/all_gather | solution.py:56
  186.8 195.1 %all-gather.11.cloned.1.call-start = ((), (), s32[]{:S(2)}) async-start(), calls=%async_computation.6 | async-start | bytes 6291456 | tf_op jit(solution)/shard_map/all_gather | solution.py:58
Sparse Core Ops, SparseCore 0:
  32.4 80.1 all-gather.4
  134.9 38.1 reduce-scatter.1
  186.4 53.9 all-gather.8
  242.3 62.6 all-gather.6
  306.9 75.0 all-gather.10
